TPU v7x, 32 devices: a whole 2x2x4 slice. The times are simulated.
32 devices in a mesh: groups: 2 (over y), pipe: 4 (over z), dp: 2 (over x), mp: 2 (over core).
Axes of the slice: x: 2, y: 2, z: 4, core: 2. Of those that a mesh axis runs over, the one named last changes fastest.
Arguments:
- latent: bfloat16 [4, 2, 2, 4, 16, 320], P(('groups', 'dp')), parts along dimension 0, may hold values from -6 to 6
- section_weight: bfloat16 [4, 2, 921600], P('pipe', None, 'mp'), may hold values from -0.01613743 to 0.01613743, as said below
- out_grad: bfloat16 [4, 2, 2, 4, 16, 320], P(('groups', 'dp')), parts along dimension 0, may hold values from -0.29882812 to 0.29882812
Outputs:
- section_grad: float32 [8, 921600], P(('groups', 'pipe'), 'mp'), parts along dimension 0
There are 2 independent parts, one for each index of `groups`. A program takes and returns all parts, laid end to end along the dimension named above; an argument that names none is the same for every part. Nothing has to cross between parts.
Inputs may be any that keep to these rules, and one draw needn't show every extreme that they name: section_weight[j, 0] equals section_weight[3 - j, 0] and section_weight[j, 1] equals section_weight[3 - j, 1] for every j: both devices of a mirrored pair hold the same two blocks.
All inputs are finite; a program needn't handle non-finite values.
Results may differ from a plain program's by a relative error of at most 0.0065.
Values may be sent and summed in bfloat16 or wider, within the bound.
No kernel may reach another device: no remote copies, remote signals or barrier semaphores. Data moves between devices by JAX's collectives and lax.ppermute only.
A program may use at most 64 MiB of HBM per device.

v0:
```python
import jax
import jax.numpy as jnp
from jax import lax
from jax.sharding import PartitionSpec as P


def shifted_2(block, axis, distance):
    devices = range(lax.axis_size(axis))
    route = [(i - distance, i) for i in devices if i - distance in devices]
    return lax.ppermute(block, axis, route)


def patches(image_in):
    img_rows, img_cols, channels = (image_in.shape[-3], image_in.shape[-2], image_in.shape[-1])
    padded = jnp.pad(image_in, [(0, 0)] * (image_in.ndim - 3) + [(1, 1), (1, 1), (0, 0)])
    shifted = [
        padded[..., row_off : row_off + img_rows, col_off : col_off + img_cols, :]
        for row_off in range(3)
        for col_off in range(3)
    ]
    return jnp.stack(shifted, axis=-2).reshape(-1, 9 * channels)


def silu_slope(pre_act):
    sigmoid = jax.nn.sigmoid(pre_act)
    return sigmoid * (1.0 + pre_act * (1.0 - sigmoid))


def mirror(payload):
    blocks = payload.reshape(lax.axis_size("pipe"), -1)
    spread = lax.all_to_all(blocks, "pipe", split_axis=0, concat_axis=0, tiled=True)
    returned = lax.all_to_all(jnp.flip(spread, 0), "pipe", split_axis=0, concat_axis=0, tiled=True)
    return returned.reshape(payload.shape)


def mirror_sums(payload):
    blocks = payload.reshape(lax.axis_size("pipe"), -1)
    spread = lax.all_to_all(blocks, "pipe", split_axis=0, concat_axis=0, tiled=True)
    returned = lax.all_to_all(jnp.flip(spread, 0), "pipe", split_axis=0, concat_axis=0, tiled=True)
    return returned.reshape(payload.shape)


def pass_on(payload, from_below):
    from_lower = shifted_2(payload, "pipe", 1)
    from_upper = shifted_2(payload, "pipe", -1)
    return (
        jnp.where(from_below, from_lower, from_upper),
        jnp.where(from_below, from_upper, from_lower),
    )


def take_slot(buffer, slot_index):
    return lax.dynamic_index_in_dim(buffer, slot_index, 0, keepdims=False)


def put_slot(buffer, payload, slot_index, active):
    return jnp.where(
        active, lax.dynamic_update_index_in_dim(buffer, payload, slot_index, 0), buffer
    )


def run_forward(source, skip_in, weight_half, position, from_below, tick_count):
    micro_count = source.shape[0]
    img_rows, img_cols, channels = (source.shape[1], source.shape[2], source.shape[3])
    chan_half = weight_half.shape[0] // (9 * channels)
    offset = lax.axis_index("mp") * chan_half
    row_weight = weight_half.reshape(chan_half, 9 * channels)

    def one_tick(tick_idx, state_carry):
        incoming, inputs, actives, outputs, crossed = state_carry
        micro_idx = tick_idx - position
        active = (micro_idx >= 0) & (micro_idx < micro_count)
        clipped = jnp.clip(micro_idx, 0, micro_count - 1)
        current = jnp.where(position == 0, take_slot(source, clipped), incoming)
        pre_act = current.astype(jnp.float32) + take_slot(skip_in, clipped).astype(jnp.float32)
        activation = jax.nn.silu(pre_act).astype(jnp.bfloat16)
        conv_out = lax.dot_general(
            patches(activation),
            row_weight,
            (((1,), (1,)), ((), ())),
            preferred_element_type=jnp.float32,
        )
        own_part = lax.dynamic_slice_in_dim(current, offset, chan_half, 2)
        output_half = (
            own_part.astype(jnp.float32) + conv_out.reshape(img_rows, img_cols, chan_half)
        ).astype(jnp.bfloat16)
        output = lax.all_gather(output_half, "mp", axis=2, tiled=True)
        chosen, other_side = pass_on(output, from_below)
        return (
            chosen,
            put_slot(inputs, current, clipped, active),
            put_slot(actives, activation, clipped, active),
            put_slot(outputs, output, clipped, active),
            put_slot(crossed, other_side, clipped, active),
        )

    initial = (
        jnp.zeros_like(source[0]),
        jnp.zeros_like(source),
        jnp.zeros_like(source),
        jnp.zeros_like(source),
        jnp.zeros_like(source),
    )
    final_state = lax.fori_loop(0, tick_count, one_tick, initial)
    return (final_state[1], final_state[2], final_state[3], final_state[4])


def run_backward(
    extra_cot, inputs, actives, skip_in, weight_half, position, from_below, tick_count, end_flag
):
    micro_count = inputs.shape[0]
    img_rows, img_cols, channels = (inputs.shape[1], inputs.shape[2], inputs.shape[3])
    chan_half = weight_half.shape[0] // (9 * channels)
    offset = lax.axis_index("mp") * chan_half
    back_weight = (
        jnp.flip(weight_half.reshape(chan_half, 3, 3, channels), (1, 2))
        .transpose(1, 2, 0, 3)
        .reshape(9 * chan_half, channels)
    )

    def one_tick(tick_idx, state_carry):
        incoming, cot_parts, skip_terms = state_carry
        micro_idx = tick_idx - position
        active = (micro_idx >= 0) & (micro_idx < micro_count)
        clipped = jnp.clip(micro_idx, 0, micro_count - 1)
        received = jnp.where(position == 0, 0.0, incoming.astype(jnp.float32))
        cotangent = (received + take_slot(extra_cot, clipped)).astype(jnp.bfloat16)
        cot_half = lax.dynamic_slice_in_dim(cotangent, offset, chan_half, 2)
        partial_value = jnp.dot(
            patches(cot_half), back_weight, preferred_element_type=jnp.float32
        ).reshape(img_rows, img_cols, channels)
        summed = lax.psum(partial_value, "mp")
        pre_act = take_slot(inputs, clipped).astype(jnp.float32) + take_slot(
            skip_in, clipped
        ).astype(jnp.float32)
        slope_term = summed * silu_slope(pre_act)
        passed = (cotangent.astype(jnp.float32) + slope_term).astype(jnp.bfloat16)
        skip_term = (slope_term + jnp.where(end_flag, passed.astype(jnp.float32), 0.0)).astype(
            jnp.bfloat16
        )
        chosen, other_side = pass_on(passed, from_below)
        return (
            chosen,
            put_slot(cot_parts, cot_half, clipped, active),
            put_slot(skip_terms, skip_term, clipped, active),
        )

    initial = (
        jnp.zeros_like(inputs[0]),
        jnp.zeros((micro_count, img_rows, img_cols, chan_half), jnp.bfloat16),
        jnp.zeros_like(inputs),
    )
    final_state = lax.fori_loop(0, tick_count, one_tick, initial)
    weight_grad = lax.dot_general(
        final_state[1].reshape(-1, chan_half),
        patches(actives),
        (((0,), (0,)), ((), ())),
        preferred_element_type=jnp.float32,
    )
    return (weight_grad.reshape(weight_half.shape), final_state[2])


def local(latent, section_weight, out_grad):
    pipe_size = lax.axis_size("pipe")
    half_size = pipe_size // 2
    device = lax.axis_index("pipe")
    lower_half = device < half_size
    upper_half = jnp.logical_not(lower_half)
    pair_index = jnp.minimum(device, pipe_size - 1 - device)
    tick_count = half_size + latent.shape[2] - 1
    encoder_weight = section_weight[0, 0]
    decoder_weight = section_weight[0, 1]
    first_dir = jnp.where(lower_half, 0, 1)
    samples = take_slot(latent[0], first_dir)
    zero_skip = jnp.zeros_like(samples)
    enc_inputs, enc_acts, enc_out, middle_in = run_forward(
        samples, zero_skip, encoder_weight, pair_index, lower_half, tick_count
    )
    skip_in = mirror(enc_out)
    dec_source = jnp.where(pair_index == half_size - 1, middle_in, skip_in)
    dec_inputs, dec_acts, dec_out, unused_in = run_forward(
        dec_source, skip_in, decoder_weight, half_size - 1 - pair_index, upper_half, tick_count
    )
    seed_cot = take_slot(out_grad[0], 1 - first_dir).astype(jnp.float32)
    seed_cot = jnp.where(pair_index == 0, seed_cot, 0.0)
    decoder_grad, dec_terms = run_backward(
        seed_cot,
        dec_inputs,
        dec_acts,
        skip_in,
        decoder_weight,
        pair_index,
        lower_half,
        tick_count,
        pair_index == half_size - 1,
    )
    terms_in = mirror(dec_terms).astype(jnp.float32)
    encoder_grad, enc_terms = run_backward(
        terms_in,
        enc_inputs,
        enc_acts,
        zero_skip,
        encoder_weight,
        half_size - 1 - pair_index,
        upper_half,
        tick_count,
        False,
    )
    kept_grad = jnp.where(lower_half, encoder_grad, decoder_grad)
    sent_grad = jnp.where(lower_half, decoder_grad, encoder_grad)
    combined = kept_grad + mirror_sums(sent_grad)
    combined = lax.psum(combined, "dp")
    return combined.reshape(1, -1)


def solution(mesh):
    return jax.shard_map(
        local,
        mesh=mesh,
        in_specs=(
            P(("groups", "dp"), None, None, None, None, None),
            P("pipe", None, "mp"),
            P(("groups", "dp"), None, None, None, None, None),
        ),
        out_specs=P(("groups", "pipe"), "mp"),
        check_vma=False,
    )
```

profile of v0, /device:TPU:0, one launch (start us, length us, event | category | flops | bytes accessed | tf_op | source)
XLA Modules:
  0.0 979.8 jit_solution(13960116564052826964)
XLA Ops:
  7.4 21.7 %slice_reduce_fusion = (bf16[460800]{0:T(1024)(128)(2,1)S(1)}, bf16[460800]{0:T(1024)(128)(2,1)}) fusion(bf16[1,2,460800]{2,1,0:T(2,128)(2,1)} %param.12), kind=kLoop, calls=%fused_computation.170 | loop fusion | bytes 3686400 | tf_op jit(solution)/shard_map/slice | solution.py:171
  31.8 46.2 %while.82 = (s32[]{:T(128)}, bf16[4,16,320]{2,1,0:T(8,128)(2,1)S(1)}, bf16[2,4,16,320]{3,2,1,0:T(8,128)(2,1)S(1)}, bf16[2,4,16,320]{3,2,1,0:T(8,128)(2,1)S(1)}, ...) while((s32[]{:T(128)}, ...), condition=%wide.region_1.2_spmd.clone, body=%wide.region_0.1_spmd.clone.sunk | while | flops 59545608 | bytes 6439339 | solution.py:104
  36.7 4.8 collective-permute-start
  85.1 5.5 all-to-all-done
  108.3 8.3 rev.18
  118.0 11.2 %rev.21 = bf16[160,3,3,320]{3,2,1,0:T(4,128)(2,1)} reverse(bf16[160,3,3,320]{3,2,1,0:T(4,128)(2,1)} %reshape_squeeze.15), dimensions={1,2} | reverse | bytes 1843200 | tf_op jit(solution)/shard_map/jit(_flip)/rev | solution.py:116
  135.4 69.2 %while.83 = (s32[]{:T(128)}, bf16[4,16,320]{1,0,2:T(4,128)(2,1)}, bf16[2,4,16,320]{3,2,1,0:T(8,128)(2,1)}, bf16[2,4,16,320]{3,2,1,0:T(8,128)(2,1)S(1)}, pred[]{:...) while((s32[]{:T(128)}, bf16[4,16,320]{1,0,2:T(4,128)(2,1)}, ...), condition=%wide.region_3.4_spmd.clone, body=%wide.region_2.3_spmd.clone.sunk | while | flops 59279368 | bytes 5611900 | solution.py:104
  148.0 5.9 collective-permute-done.2
  170.9 5.9 collective-permute-done.2
  193.8 5.9 collective-permute-done.2
  205.7 95.1 %while.84 = (s32[]{:T(128)}, bf16[4,16,320]{2,1,0:T(8,128)(2,1)}, bf16[2,4,16,160]{3,2,1,0:T(8,128)(2,1)S(1)}, bf16[2,4,16,320]{3,2,1,0:T(8,128)(2,1)S(1)}, pred...) while((s32[]{:T(128)}, bf16[4,16,320]{2,1,0:T(8,128)(2,1)}, ...), condition=%wide.region_6.7_spmd.clone, body=%wide.region_4.6_spmd.clone.sunk | while | flops 59811848 | bytes 4673925 | solution.py:153
  208.8 16.3 %all-reduce.12.cloned.1.call-done = f32[4,16,320]{2,1,0:T(8,128)} async-done(((f32[4,16,320]{2,1,0:T(8,128)}), f32[4,16,320]{2,1,0:T(8,128)}) %all-reduce.12.cloned.1.call-update) | async-done | bytes 81936 | tf_op jit(solution)/shard_map/while/body/eval_jaxpr/psum | solution.py:132
  239.2 18.1 %all-reduce.12.cloned.1.call-done = f32[4,16,320]{2,1,0:T(8,128)} async-done(((f32[4,16,320]{2,1,0:T(8,128)}), f32[4,16,320]{2,1,0:T(8,128)}) %all-reduce.12.cloned.1.call-update) | async-done | bytes 81936 | tf_op jit(solution)/shard_map/while/body/eval_jaxpr/psum | solution.py:132
  271.5 18.1 %all-reduce.12.cloned.1.call-done = f32[4,16,320]{2,1,0:T(8,128)} async-done(((f32[4,16,320]{2,1,0:T(8,128)}), f32[4,16,320]{2,1,0:T(8,128)}) %all-reduce.12.cloned.1.call-update) | async-done | bytes 81936 | tf_op jit(solution)/shard_map/while/body/eval_jaxpr/psum | solution.py:132
  325.6 94.5 %while.85 = (s32[]{:T(128)}, bf16[4,16,320]{2,1,0:T(8,128)(2,1)S(1)}, bf16[2,4,16,160]{3,2,1,0:T(8,128)(2,1)S(1)}, pred[]{:T(512)}, pred[]{:T(512)}, /*index=5*/...) while((s32[]{:T(128)}, ...), condition=%wide.region_9.10_spmd.clone, body=%wide.region_7.9_spmd.clone.sunk | while | flops 59381768 | bytes 3977547 | solution.py:153
  327.7 19.0 %all-reduce.14.cloned.1.call-done = f32[4,16,320]{2,1,0:T(8,128)} async-done(((f32[4,16,320]{2,1,0:T(8,128)}), f32[4,16,320]{2,1,0:T(8,128)}) %all-reduce.14.cloned.1.call-update) | async-done | bytes 81936 | tf_op jit(solution)/shard_map/while/body/eval_jaxpr/psum | solution.py:132
  359.5 18.7 %all-reduce.14.cloned.1.call-done = f32[4,16,320]{2,1,0:T(8,128)} async-done(((f32[4,16,320]{2,1,0:T(8,128)}), f32[4,16,320]{2,1,0:T(8,128)}) %all-reduce.14.cloned.1.call-update) | async-done | bytes 81936 | tf_op jit(solution)/shard_map/while/body/eval_jaxpr/psum | solution.py:132
  390.8 18.7 %all-reduce.14.cloned.1.call-done = f32[4,16,320]{2,1,0:T(8,128)} async-done(((f32[4,16,320]{2,1,0:T(8,128)}), f32[4,16,320]{2,1,0:T(8,128)}) %all-reduce.14.cloned.1.call-update) | async-done | bytes 81936 | tf_op jit(solution)/shard_map/while/body/eval_jaxpr/psum | solution.py:132
  422.9 4.7 select_n.488
  427.7 45.6 %all_to_all.62 = f32[4,1,115200]{2,1,0:T(1,128)S(1)} all-to-all(f32[4,1,115200]{2,1,0:T(1,128)} %select_n.488), channel_id=1, replica_groups=mesh['groups'=2,'pipe'=4,'dp'=2,'mp'=2] {'pipe'}, dimensions={0} | all-to-all | bytes 3686400 | tf_op jit(solution)/shard_map/all_to_all | solution.py:38
  475.0 383.0 %rev.22 = f32[4,115200]{1,0:T(4,128)} reverse(f32[4,115200]{1,0:T(4,128)} %bitcast.459), dimensions={0} | reverse | bytes 3686400 | tf_op jit(solution)/shard_map/jit(_flip)/rev | solution.py:39
  858.0 4.7 copy.61
  869.4 39.5 %all-to-all-done.5 = f32[4,1,115200]{2,1,0:T(1,128)} async-done(((f32[4,1,115200]{2,1,0:T(1,128)}), f32[4,1,115200]{2,1,0:T(1,128)}, u32[]{:S(2)}, u32[]{:S(2)}) %all-to-all-start.5) | async-done | bytes 1843232 | tf_op jit(solution)/shard_map/all_to_all | solution.py:39
  912.3 56.3 %all-reduce.10.cloned.1.call-done = f32[1,460800]{1,0:T(1,128)} async-done(((f32[1,460800]{1,0:T(1,128)}), f32[1,460800]{1,0:T(1,128)}) %all-reduce.10.cloned.1.call-update) | async-done | bytes 1843216 | tf_op jit(solution)/shard_map/psum | solution.py:212
  (427 shorter events, 251.1 us)
Async XLA Ops:
  36.7 6.6 collective-permute-start
  41.5 6.0 collective-permute-start.1
  56.4 6.0 collective-permute-start.1
  71.4 6.0 collective-permute-start.1
  81.5 9.1 all-to-all-start
  94.2 39.2 %all-to-all-start.1 = ((bf16[4,2,5120]{2,1,0:T(2,128)(2,1)}), bf16[4,2,5120]{2,1,0:T(2,128)(2,1)S(1)}, u32[]{:S(2)}, u32[]{:S(2)}) async-start(bf16[4,2,5120]{2,1,0:T(2,128)(2,1)} %reshape.168), calls=%async_computation.1 | async-start | bytes 163840 | tf_op jit(solution)/shard_map/all_to_all | solution.py:32
  142.9 11.0 %collective-permute-start.2 = (bf16[4,16,320]{1,0,2:T(4,128)(2,1)S(1)}, bf16[4,16,320]{1,0,2:T(4,128)(2,1)S(1)}, u32[]{:S(2)}, u32[]{:S(2)}) collective-permute-start(bf16[4,16,320]{1,0,2:T(4,128)(2,1)S(1)} %all_gather.25), channel_id=1, source_target_pairs={{0,4},{4,8},{8,12},{1,5},{5,9},{9,13},{2,6},{6,10},{10,14},{3,7},{... | collective-permute-start | bytes 122888 | tf_op jit(solution)/shard_map/while/body/eval_jaxpr/ppermute | solution.py:10
  146.6 11.4 %collective-permute-start.3 = (bf16[4,16,320]{1,0,2:T(4,128)(2,1)S(1)}, bf16[4,16,320]{1,0,2:T(4,128)(2,1)S(1)}, u32[]{:S(2)}, u32[]{:S(2)}) collective-permute-start(bf16[4,16,320]{1,0,2:T(4,128)(2,1)S(1)} %all_gather.25), channel_id=1, source_target_pairs={{4,0},{8,4},{12,8},{5,1},{9,5},{13,9},{6,2},{10,6},{14,10},{7,3},{... | collective-permute-start | bytes 122888 | tf_op jit(solution)/shard_map/while/body/eval_jaxpr/ppermute | solution.py:10
  166.2 10.6 %collective-permute-start.2 = (bf16[4,16,320]{1,0,2:T(4,128)(2,1)S(1)}, bf16[4,16,320]{1,0,2:T(4,128)(2,1)S(1)}, u32[]{:S(2)}, u32[]{:S(2)}) collective-permute-start(bf16[4,16,320]{1,0,2:T(4,128)(2,1)S(1)} %all_gather.25), channel_id=1, source_target_pairs={{0,4},{4,8},{8,12},{1,5},{5,9},{9,13},{2,6},{6,10},{10,14},{3,7},{... | collective-permute-start | bytes 122888 | tf_op jit(solution)/shard_map/while/body/eval_jaxpr/ppermute | solution.py:10
  169.5 11.4 %collective-permute-start.3 = (bf16[4,16,320]{1,0,2:T(4,128)(2,1)S(1)}, bf16[4,16,320]{1,0,2:T(4,128)(2,1)S(1)}, u32[]{:S(2)}, u32[]{:S(2)}) collective-permute-start(bf16[4,16,320]{1,0,2:T(4,128)(2,1)S(1)} %all_gather.25), channel_id=1, source_target_pairs={{4,0},{8,4},{12,8},{5,1},{9,5},{13,9},{6,2},{10,6},{14,10},{7,3},{... | collective-permute-start | bytes 122888 | tf_op jit(solution)/shard_map/while/body/eval_jaxpr/ppermute | solution.py:10
  189.1 10.6 %collective-permute-start.2 = (bf16[4,16,320]{1,0,2:T(4,128)(2,1)S(1)}, bf16[4,16,320]{1,0,2:T(4,128)(2,1)S(1)}, u32[]{:S(2)}, u32[]{:S(2)}) collective-permute-start(bf16[4,16,320]{1,0,2:T(4,128)(2,1)S(1)} %all_gather.25), channel_id=1, source_target_pairs={{0,4},{4,8},{8,12},{1,5},{5,9},{9,13},{2,6},{6,10},{10,14},{3,7},{... | collective-permute-start | bytes 122888 | tf_op jit(solution)/shard_map/while/body/eval_jaxpr/ppermute | solution.py:10
  192.5 11.4 %collective-permute-start.3 = (bf16[4,16,320]{1,0,2:T(4,128)(2,1)S(1)}, bf16[4,16,320]{1,0,2:T(4,128)(2,1)S(1)}, u32[]{:S(2)}, u32[]{:S(2)}) collective-permute-start(bf16[4,16,320]{1,0,2:T(4,128)(2,1)S(1)} %all_gather.25), channel_id=1, source_target_pairs={{4,0},{8,4},{12,8},{5,1},{9,5},{13,9},{6,2},{10,6},{14,10},{7,3},{... | collective-permute-start | bytes 122888 | tf_op jit(solution)/shard_map/while/body/eval_jaxpr/ppermute | solution.py:10
  205.7 19.3 %all-reduce.12.cloned.1.call-start = ((), (), s32[]{:S(2)}) async-start(), calls=%async_computation.7 | async-start | bytes 196608 | tf_op jit(solution)/shard_map/while/body/eval_jaxpr/psum | solution.py:132
  229.6 6.0 collective-permute-start.5
  236.2 21.1 %all-reduce.12.cloned.1.call-start = ((), (), s32[]{:S(2)}) async-start(), calls=%async_computation.7 | async-start | bytes 196608 | tf_op jit(solution)/shard_map/while/body/eval_jaxpr/psum | solution.py:132
  261.9 6.0 collective-permute-start.5
  268.5 21.1 %all-reduce.12.cloned.1.call-start = ((), (), s32[]{:S(2)}) async-start(), calls=%async_computation.7 | async-start | bytes 196608 | tf_op jit(solution)/shard_map/while/body/eval_jaxpr/psum | solution.py:132
  302.8 9.5 all-to-all-start.2
  315.8 9.1 all-to-all-start.3
  325.6 21.1 %all-reduce.14.cloned.1.call-start = ((), (), s32[]{:S(2)}) async-start(), calls=%async_computation.8 | async-start | bytes 196608 | tf_op jit(solution)/shard_map/while/body/eval_jaxpr/psum | solution.py:132
  357.4 20.8 %all-reduce.14.cloned.1.call-start = ((), (), s32[]{:S(2)}) async-start(), calls=%async_computation.8 | async-start | bytes 196608 | tf_op jit(solution)/shard_map/while/body/eval_jaxpr/psum | solution.py:132
  388.7 20.8 %all-reduce.14.cloned.1.call-start = ((), (), s32[]{:S(2)}) async-start(), calls=%async_computation.8 | async-start | bytes 196608 | tf_op jit(solution)/shard_map/while/body/eval_jaxpr/psum | solution.py:132
  862.7 46.2 %all-to-all-start.5 = ((f32[4,1,115200]{2,1,0:T(1,128)}), f32[4,1,115200]{2,1,0:T(1,128)}, u32[]{:S(2)}, u32[]{:S(2)}) async-start(f32[4,1,115200]{2,1,0:T(1,128)} %copy.61), calls=%async_computation.5 | async-start | bytes 3686400 | tf_op jit(solution)/shard_map/all_to_all | solution.py:39
  867.1 101.6 %all-reduce.10.cloned.1.call-start = ((), (), s32[]{:S(2)}) async-start(), calls=%async_computation.6 | async-start | bytes 3686400 | tf_op jit(solution)/shard_map/psum | solution.py:212
  (47 other events, 466.7 us)
Sparse Core Ops, SparseCore 0:
  209.0 16.0 all-reduce.11
  239.5 17.7 all-reduce.11
  271.7 17.7 all-reduce.11
  328.5 18.1 all-reduce.13
  360.3 17.7 all-reduce.13
  391.7 17.7 all-reduce.13
Sparse Core Ops, SparseCore 1:
  912.4 56.2 all-reduce.9
where the time goes:
time: 997 us; the launch traced here: 980 us
  local copies, waits for them, and re-layouts  493 us (49%)
  waiting for transfers between devices  284 us (28%)
  starting transfers between devices  78.3 us (8%)
  blocking collectives  58 us (6%)
  other arithmetic  34.1 us (3%)
  between operations  15.3 us (2%)
  matrix products  14.9 us (1%)
    rev x1, local copies, waits for them, and re-layouts, mirror_sums(): jnp.flip(spread, 0)  383 us
    psum x6, waiting for transfers between devices, one_tick(): summed = lax.psum(partial_value, 'mp')  109 us
    ppermute x24, waiting for transfers between devices, shifted_2(): return lax.ppermute(block, axis, route)  69 us
    ppermute x24, starting transfers between devices, shifted_2(): return lax.ppermute(block, axis, route)  59.7 us
    psum x1, waiting for transfers between devices, local(): combined = lax.psum(combined, 'dp')  56.3 us
    all_to_all x1, blocking collectives, mirror_sums(): lax.all_to_all(blocks, 'pipe', split_axis=0, concat_axis=0, tiled=True)  45.6 us
    all_to_all x1, waiting for transfers between devices, mirror_sums(): lax.all_to_all(jnp.flip(spread, 0), 'pipe', split_axis=0, concat_axis=0,...  39.5 us
    slice x1, local copies, waits for them, and re-layouts, local(): encoder_weight = section_weight[0, 0]  21.7 us
  transfers between devices with their start and end apart: 36, of which 32 were waited for; matrix products, arithmetic and copies ran while one was open for 5% of the time, Pallas kernels for 0%

commit v1 on v0

--- a/solution.py
+++ b/solution.py
@@ -2,6 +2,17 @@
 import jax.numpy as jnp
 from jax import lax
 from jax.sharding import PartitionSpec as P
+
+
+def split_up(shard, dim, size):
+    before, after = (shard.shape[:dim], shard.shape[dim + 1 :])
+    return jnp.moveaxis(shard.reshape(*before, size, -1, *after), dim, 0)
+
+
+def joined_along(blocks, dim):
+    blocks = jnp.moveaxis(blocks, 0, dim)
+    shape = blocks.shape
+    return blocks.reshape(*shape[:dim], shape[dim] * shape[dim + 1], *shape[dim + 2 :])
 
 
 def shifted_2(block, axis, distance):
@@ -35,7 +46,14 @@
 
 def mirror_sums(payload):
     blocks = payload.reshape(lax.axis_size("pipe"), -1)
-    spread = lax.all_to_all(blocks, "pipe", split_axis=0, concat_axis=0, tiled=True)
+    peers, index = (lax.axis_size("pipe"), lax.axis_index("pipe"))
+    blocks_2 = split_up(blocks, 0, peers)
+    finished = [blocks_2[index]]
+    for turn in range(1, peers):
+        sent = blocks_2[index ^ turn]
+        finished.append(lax.ppermute(sent, "pipe", [(i_2, i_2 ^ turn) for i_2 in range(peers)]))
+    blocks_2 = jnp.stack(finished)[index ^ jnp.arange(peers)]
+    spread = joined_along(blocks_2, 0)
     returned = lax.all_to_all(jnp.flip(spread, 0), "pipe", split_axis=0, concat_axis=0, tiled=True)
     return returned.reshape(payload.shape)
 

time: 997 us -> 927 us (0.930)
  local copies, waits for them, and re-layouts: 493 us -> 428 us
  blocking collectives: 58 us -> 12.3 us
  waiting for transfers between devices: 284 us -> 315 us
  starting transfers between devices: 78.3 us -> 88.6 us
    rev x1 -> x0, local copies, waits for them, and re-layouts: 383 us -> none  [mirror_sums(): jnp.flip(spread, 0)]
    unnamed x52 -> x54, local copies, waits for them, and re-layouts: 14.8 us -> 329 us
    all_to_all x1 -> x0, blocking collectives: 45.6 us -> none  [mirror_sums(): lax.all_to_all(blocks, 'pipe', split_axis=0, concat_axis=0, tiled=True)]
    ppermute x0 -> x3, waiting for transfers between devices: none -> 31.2 us  [mirror_sums(): lax.ppermute(sent, 'pipe', [(i_2, i_2 ^ turn) for i_2 in range(peers)])]
  transfers between devices with their start and end apart: 36 -> 39, of which waited for: 32 -> 34; matrix products, arithmetic and copies ran while one was open for 5% -> 5% of each run, Pallas kernels for 0% -> 0%
where the time goes in v1:
time: 927 us; the launch traced here: 912 us
  local copies, waits for them, and re-layouts  428 us (46%)
  waiting for transfers between devices  315 us (34%)
  starting transfers between devices  88.6 us (10%)
  other arithmetic  36.2 us (4%)
  between operations  15.3 us (2%)
  matrix products  14.9 us (2%)
  blocking collectives  12.3 us (1%)
    unnamed x54, local copies, waits for them, and re-layouts  329 us
    psum x6, waiting for transfers between devices, one_tick(): summed = lax.psum(partial_value, 'mp')  109 us
    ppermute x24, waiting for transfers between devices, shifted_2(): return lax.ppermute(block, axis, route)  69 us
    ppermute x24, starting transfers between devices, shifted_2(): return lax.ppermute(block, axis, route)  59.7 us
    psum x1, waiting for transfers between devices, local(): combined = lax.psum(combined, 'dp')  56.3 us
    all_to_all x1, waiting for transfers between devices, mirror_sums(): lax.all_to_all(jnp.flip(spread, 0), 'pipe', split_axis=0, concat_axis=0,...  39.2 us
    ppermute x3, waiting for transfers between devices, mirror_sums(): lax.ppermute(sent, 'pipe', [(i_2, i_2 ^ turn) for i_2 in range(peers)])  31.2 us
    slice x1, local copies, waits for them, and re-layouts, local(): encoder_weight = section_weight[0, 0]  21.7 us
  transfers between devices with their start and end apart: 39, of which 34 were waited for; matrix products, arithmetic and copies ran while one was open for 5% of the time, Pallas kernels for 0%

profile of v1, /device:TPU:0, one launch (start us, length us, event | category | flops | bytes accessed | tf_op | source)
XLA Modules:
  0.0 912.2 jit_solution(10739663174352963998)
XLA Ops:
  7.4 21.7 %slice_reduce_fusion = (bf16[460800]{0:T(1024)(128)(2,1)S(1)}, bf16[460800]{0:T(1024)(128)(2,1)}) fusion(bf16[1,2,460800]{2,1,0:T(2,128)(2,1)} %param.12), kind=kLoop, calls=%fused_computation.171 | loop fusion | bytes 3686400 | tf_op jit(solution)/shard_map/slice | solution.py:189
  31.9 46.3 %while.82 = (s32[]{:T(128)}, bf16[4,16,320]{2,1,0:T(8,128)(2,1)S(1)}, bf16[2,4,16,320]{3,2,1,0:T(8,128)(2,1)S(1)}, bf16[2,4,16,320]{3,2,1,0:T(8,128)(2,1)S(1)}, ...) while((s32[]{:T(128)}, ...), condition=%wide.region_1.2_spmd.clone, body=%wide.region_0.1_spmd.clone.sunk | while | flops 59545608 | bytes 6439339 | solution.py:122
  85.3 5.5 all-to-all-done
  108.6 8.3 rev.18
  118.2 11.2 %rev.21 = bf16[160,3,3,320]{3,2,1,0:T(4,128)(2,1)} reverse(bf16[160,3,3,320]{3,2,1,0:T(4,128)(2,1)} %reshape_squeeze.15), dimensions={1,2} | reverse | bytes 1843200 | tf_op jit(solution)/shard_map/jit(_flip)/rev | solution.py:134
  135.7 69.3 %while.83 = (s32[]{:T(128)}, bf16[4,16,320]{1,0,2:T(4,128)(2,1)}, bf16[2,4,16,320]{3,2,1,0:T(8,128)(2,1)}, bf16[2,4,16,320]{3,2,1,0:T(8,128)(2,1)S(1)}, pred[]{:...) while((s32[]{:T(128)}, bf16[4,16,320]{1,0,2:T(4,128)(2,1)}, ...), condition=%wide.region_3.4_spmd.clone, body=%wide.region_2.3_spmd.clone.sunk | while | flops 59279368 | bytes 5611900 | solution.py:122
  148.2 5.9 collective-permute-done.2
  171.2 5.9 collective-permute-done.2
  194.2 5.9 collective-permute-done.2
  206.1 95.1 %while.84 = (s32[]{:T(128)}, bf16[4,16,320]{2,1,0:T(8,128)(2,1)}, bf16[2,4,16,160]{3,2,1,0:T(8,128)(2,1)S(1)}, bf16[2,4,16,320]{3,2,1,0:T(8,128)(2,1)S(1)}, pred...) while((s32[]{:T(128)}, bf16[4,16,320]{2,1,0:T(8,128)(2,1)}, ...), condition=%wide.region_6.7_spmd.clone, body=%wide.region_4.6_spmd.clone.sunk | while | flops 59811848 | bytes 4673925 | solution.py:171
  209.1 16.3 %all-reduce.12.cloned.1.call-done = f32[4,16,320]{2,1,0:T(8,128)} async-done(((f32[4,16,320]{2,1,0:T(8,128)}), f32[4,16,320]{2,1,0:T(8,128)}) %all-reduce.12.cloned.1.call-update) | async-done | bytes 81936 | tf_op jit(solution)/shard_map/while/body/eval_jaxpr/psum | solution.py:150
  239.6 18.1 %all-reduce.12.cloned.1.call-done = f32[4,16,320]{2,1,0:T(8,128)} async-done(((f32[4,16,320]{2,1,0:T(8,128)}), f32[4,16,320]{2,1,0:T(8,128)}) %all-reduce.12.cloned.1.call-update) | async-done | bytes 81936 | tf_op jit(solution)/shard_map/while/body/eval_jaxpr/psum | solution.py:150
  271.9 18.1 %all-reduce.12.cloned.1.call-done = f32[4,16,320]{2,1,0:T(8,128)} async-done(((f32[4,16,320]{2,1,0:T(8,128)}), f32[4,16,320]{2,1,0:T(8,128)}) %all-reduce.12.cloned.1.call-update) | async-done | bytes 81936 | tf_op jit(solution)/shard_map/while/body/eval_jaxpr/psum | solution.py:150
  326.1 94.5 %while.85 = (s32[]{:T(128)}, bf16[4,16,320]{2,1,0:T(8,128)(2,1)S(1)}, bf16[2,4,16,160]{3,2,1,0:T(8,128)(2,1)S(1)}, pred[]{:T(512)}, pred[]{:T(512)}, /*index=5*/...) while((s32[]{:T(128)}, ...), condition=%wide.region_9.10_spmd.clone, body=%wide.region_7.9_spmd.clone.sunk | while | flops 59381768 | bytes 3977547 | solution.py:171
  328.2 19.0 %all-reduce.14.cloned.1.call-done = f32[4,16,320]{2,1,0:T(8,128)} async-done(((f32[4,16,320]{2,1,0:T(8,128)}), f32[4,16,320]{2,1,0:T(8,128)}) %all-reduce.14.cloned.1.call-update) | async-done | bytes 81936 | tf_op jit(solution)/shard_map/while/body/eval_jaxpr/psum | solution.py:150
  359.9 18.6 %all-reduce.14.cloned.1.call-done = f32[4,16,320]{2,1,0:T(8,128)} async-done(((f32[4,16,320]{2,1,0:T(8,128)}), f32[4,16,320]{2,1,0:T(8,128)}) %all-reduce.14.cloned.1.call-update) | async-done | bytes 81936 | tf_op jit(solution)/shard_map/while/body/eval_jaxpr/psum | solution.py:150
  391.3 18.6 %all-reduce.14.cloned.1.call-done = f32[4,16,320]{2,1,0:T(8,128)} async-done(((f32[4,16,320]{2,1,0:T(8,128)}), f32[4,16,320]{2,1,0:T(8,128)}) %all-reduce.14.cloned.1.call-update) | async-done | bytes 81936 | tf_op jit(solution)/shard_map/while/body/eval_jaxpr/psum | solution.py:150
  425.7 5.1 constant_dynamic-slice_fusion.2
  435.3 15.5 %collective-permute-done.8 = f32[1,115200]{1,0:T(1,128)S(1)} collective-permute-done((f32[1,115200]{1,0:T(1,128)S(1)}, f32[1,115200]{1,0:T(1,128)S(1)}, u32[]{:S(2)}, u32[]{:S(2)}) %collective-permute-start.8) | collective-permute-done | bytes 460832 | tf_op jit(solution)/shard_map/ppermute | solution.py:54
  450.8 15.7 %collective-permute-done.9 = f32[1,115200]{1,0:T(1,128)S(1)} collective-permute-done((f32[1,115200]{1,0:T(1,128)S(1)}, f32[1,115200]{1,0:T(1,128)S(1)}, u32[]{:S(2)}, u32[]{:S(2)}) %collective-permute-start.9) | collective-permute-done | bytes 460832 | tf_op jit(solution)/shard_map/ppermute | solution.py:54
  470.8 315.5 %reverse = f32[4,115200]{1,0:T(4,128)S(1)} reverse(f32[4,115200]{1,0:T(4,128)} %gather_fusion), dimensions={0} | reverse | bytes 3686400
  789.5 10.4 %all-to-all-start.4 = ((f32[4,1,115200]{2,1,0:T(1,128)}), f32[4,1,115200]{2,1,0:T(1,128)}, u32[]{:S(2)}, u32[]{:S(2)}) async-start(f32[4,1,115200]{2,1,0:T(1,128)} %copy.59), calls=%async_computation.4 | async-start | bytes 3686400 | tf_op jit(solution)/shard_map/all_to_all | solution.py:57
  802.1 39.2 %all-to-all-done.4 = f32[4,1,115200]{2,1,0:T(1,128)} async-done(((f32[4,1,115200]{2,1,0:T(1,128)}), f32[4,1,115200]{2,1,0:T(1,128)}, u32[]{:S(2)}, u32[]{:S(2)}) %all-to-all-start.4) | async-done | bytes 1843232 | tf_op jit(solution)/shard_map/all_to_all | solution.py:57
  844.8 56.3 %all-reduce.10.cloned.1.call-done = f32[1,460800]{1,0:T(1,128)} async-done(((f32[1,460800]{1,0:T(1,128)}), f32[1,460800]{1,0:T(1,128)}) %all-reduce.10.cloned.1.call-update) | async-done | bytes 1843216 | tf_op jit(solution)/shard_map/psum | solution.py:230
  (438 shorter events, 264.4 us)
Async XLA Ops:
  36.7 6.6 collective-permute-start
  71.5 6.0 collective-permute-start.1
  81.7 9.1 all-to-all-start
  94.4 39.3 %all-to-all-start.1 = ((bf16[4,2,5120]{2,1,0:T(2,128)(2,1)}), bf16[4,2,5120]{2,1,0:T(2,128)(2,1)S(1)}, u32[]{:S(2)}, u32[]{:S(2)}) async-start(bf16[4,2,5120]{2,1,0:T(2,128)(2,1)} %reshape.196), calls=%async_computation.1 | async-start | bytes 163840 | tf_op jit(solution)/shard_map/all_to_all | solution.py:43
  143.2 11.0 %collective-permute-start.2 = (bf16[4,16,320]{1,0,2:T(4,128)(2,1)S(1)}, bf16[4,16,320]{1,0,2:T(4,128)(2,1)S(1)}, u32[]{:S(2)}, u32[]{:S(2)}) collective-permute-start(bf16[4,16,320]{1,0,2:T(4,128)(2,1)S(1)} %all_gather.25), channel_id=1, source_target_pairs={{0,4},{4,8},{8,12},{1,5},{5,9},{9,13},{2,6},{6,10},{10,14},{3,7},{... | collective-permute-start | bytes 122888 | tf_op jit(solution)/shard_map/while/body/eval_jaxpr/ppermute | solution.py:21
  146.9 11.4 %collective-permute-start.3 = (bf16[4,16,320]{1,0,2:T(4,128)(2,1)S(1)}, bf16[4,16,320]{1,0,2:T(4,128)(2,1)S(1)}, u32[]{:S(2)}, u32[]{:S(2)}) collective-permute-start(bf16[4,16,320]{1,0,2:T(4,128)(2,1)S(1)} %all_gather.25), channel_id=1, source_target_pairs={{4,0},{8,4},{12,8},{5,1},{9,5},{13,9},{6,2},{10,6},{14,10},{7,3},{... | collective-permute-start | bytes 122888 | tf_op jit(solution)/shard_map/while/body/eval_jaxpr/ppermute | solution.py:21
  166.5 10.6 %collective-permute-start.2 = (bf16[4,16,320]{1,0,2:T(4,128)(2,1)S(1)}, bf16[4,16,320]{1,0,2:T(4,128)(2,1)S(1)}, u32[]{:S(2)}, u32[]{:S(2)}) collective-permute-start(bf16[4,16,320]{1,0,2:T(4,128)(2,1)S(1)} %all_gather.25), channel_id=1, source_target_pairs={{0,4},{4,8},{8,12},{1,5},{5,9},{9,13},{2,6},{6,10},{10,14},{3,7},{... | collective-permute-start | bytes 122888 | tf_op jit(solution)/shard_map/while/body/eval_jaxpr/ppermute | solution.py:21
  169.9 11.4 %collective-permute-start.3 = (bf16[4,16,320]{1,0,2:T(4,128)(2,1)S(1)}, bf16[4,16,320]{1,0,2:T(4,128)(2,1)S(1)}, u32[]{:S(2)}, u32[]{:S(2)}) collective-permute-start(bf16[4,16,320]{1,0,2:T(4,128)(2,1)S(1)} %all_gather.25), channel_id=1, source_target_pairs={{4,0},{8,4},{12,8},{5,1},{9,5},{13,9},{6,2},{10,6},{14,10},{7,3},{... | collective-permute-start | bytes 122888 | tf_op jit(solution)/shard_map/while/body/eval_jaxpr/ppermute | solution.py:21
  189.5 10.6 %collective-permute-start.2 = (bf16[4,16,320]{1,0,2:T(4,128)(2,1)S(1)}, bf16[4,16,320]{1,0,2:T(4,128)(2,1)S(1)}, u32[]{:S(2)}, u32[]{:S(2)}) collective-permute-start(bf16[4,16,320]{1,0,2:T(4,128)(2,1)S(1)} %all_gather.25), channel_id=1, source_target_pairs={{0,4},{4,8},{8,12},{1,5},{5,9},{9,13},{2,6},{6,10},{10,14},{3,7},{... | collective-permute-start | bytes 122888 | tf_op jit(solution)/shard_map/while/body/eval_jaxpr/ppermute | solution.py:21
  192.8 11.4 %collective-permute-start.3 = (bf16[4,16,320]{1,0,2:T(4,128)(2,1)S(1)}, bf16[4,16,320]{1,0,2:T(4,128)(2,1)S(1)}, u32[]{:S(2)}, u32[]{:S(2)}) collective-permute-start(bf16[4,16,320]{1,0,2:T(4,128)(2,1)S(1)} %all_gather.25), channel_id=1, source_target_pairs={{4,0},{8,4},{12,8},{5,1},{9,5},{13,9},{6,2},{10,6},{14,10},{7,3},{... | collective-permute-start | bytes 122888 | tf_op jit(solution)/shard_map/while/body/eval_jaxpr/ppermute | solution.py:21
  206.1 19.3 %all-reduce.12.cloned.1.call-start = ((), (), s32[]{:S(2)}) async-start(), calls=%async_computation.6 | async-start | bytes 196608 | tf_op jit(solution)/shard_map/while/body/eval_jaxpr/psum | solution.py:150
  236.6 21.1 %all-reduce.12.cloned.1.call-start = ((), (), s32[]{:S(2)}) async-start(), calls=%async_computation.6 | async-start | bytes 196608 | tf_op jit(solution)/shard_map/while/body/eval_jaxpr/psum | solution.py:150
  268.9 21.1 %all-reduce.12.cloned.1.call-start = ((), (), s32[]{:S(2)}) async-start(), calls=%async_computation.6 | async-start | bytes 196608 | tf_op jit(solution)/shard_map/while/body/eval_jaxpr/psum | solution.py:150
  294.6 6.0 collective-permute-start.5
  303.2 9.5 %all-to-all-start.2 = ((bf16[4,2,5120]{2,1,0:T(2,128)(2,1)}), bf16[4,2,5120]{2,1,0:T(2,128)(2,1)S(1)}, u32[]{:S(2)}, u32[]{:S(2)}) async-start(bf16[4,2,5120]{2,1,0:T(2,128)(2,1)} %reshape.198), calls=%async_computation.2 | async-start | bytes 163840 | tf_op jit(solution)/shard_map/all_to_all | solution.py:42
  316.3 9.1 all-to-all-start.3
  326.1 21.1 %all-reduce.14.cloned.1.call-start = ((), (), s32[]{:S(2)}) async-start(), calls=%async_computation.7 | async-start | bytes 196608 | tf_op jit(solution)/shard_map/while/body/eval_jaxpr/psum | solution.py:150
  357.8 20.8 %all-reduce.14.cloned.1.call-start = ((), (), s32[]{:S(2)}) async-start(), calls=%async_computation.7 | async-start | bytes 196608 | tf_op jit(solution)/shard_map/while/body/eval_jaxpr/psum | solution.py:150
  389.2 20.8 %all-reduce.14.cloned.1.call-start = ((), (), s32[]{:S(2)}) async-start(), calls=%async_computation.7 | async-start | bytes 196608 | tf_op jit(solution)/shard_map/while/body/eval_jaxpr/psum | solution.py:150
  430.8 20.0 %collective-permute-start.8 = (f32[1,115200]{1,0:T(1,128)S(1)}, f32[1,115200]{1,0:T(1,128)S(1)}, u32[]{:S(2)}, u32[]{:S(2)}) collective-permute-start(f32[1,115200]{1,0:T(1,128)S(1)} %get-tuple-element.1398), channel_id=1, source_target_pairs={{0,4},{4,0},{8,12},{12,8},{1,5},{5,1},{9,13},{13,9},{2,6},{6,2},{1... | collective-permute-start | bytes 1382408 | tf_op jit(solution)/shard_map/ppermute | solution.py:54
  432.3 34.2 %collective-permute-start.9 = (f32[1,115200]{1,0:T(1,128)S(1)}, f32[1,115200]{1,0:T(1,128)S(1)}, u32[]{:S(2)}, u32[]{:S(2)}) collective-permute-start(f32[1,115200]{1,0:T(1,128)S(1)} %get-tuple-element.1397), channel_id=1, source_target_pairs={{0,8},{4,12},{8,0},{12,4},{1,9},{5,13},{9,1},{13,5},{2,10},{6,14},... | collective-permute-start | bytes 1382408 | tf_op jit(solution)/shard_map/ppermute | solution.py:54
  433.3 33.2 %collective-permute-start.10 = (f32[1,115200]{1,0:T(1,128)S(1)}, f32[1,115200]{1,0:T(1,128)S(1)}, u32[]{:S(2)}, u32[]{:S(2)}) collective-permute-start(f32[1,115200]{1,0:T(1,128)S(1)} %get-tuple-element.1396), channel_id=1, source_target_pairs={{0,12},{4,8},{8,4},{12,0},{1,13},{5,9},{9,5},{13,1},{2,14},{6,10},... | collective-permute-start | bytes 1382408 | tf_op jit(solution)/shard_map/ppermute | solution.py:54
  789.5 51.8 %all-to-all-start.4 = ((f32[4,1,115200]{2,1,0:T(1,128)}), f32[4,1,115200]{2,1,0:T(1,128)}, u32[]{:S(2)}, u32[]{:S(2)}) async-start(f32[4,1,115200]{2,1,0:T(1,128)} %copy.59), calls=%async_computation.4 | async-start | bytes 3686400 | tf_op jit(solution)/shard_map/all_to_all | solution.py:57
  799.9 101.3 %all-reduce.10.cloned.1.call-start = ((), (), s32[]{:S(2)}) async-start(), calls=%async_computation.5 | async-start | bytes 3686400 | tf_op jit(solution)/shard_map/psum | solution.py:230
  (51 other events, 495.5 us)
Sparse Core Ops, SparseCore 0:
  209.3 16.0 all-reduce.11
  239.9 17.7 all-reduce.11
  272.1 17.7 all-reduce.11
  329.0 18.1 all-reduce.13
  360.8 17.7 all-reduce.13
  392.1 17.7 all-reduce.13
Sparse Core Ops, SparseCore 1:
  844.9 56.1 all-reduce.9
